TPU v7x, 32 devices: a whole 2x2x4 slice. The times are simulated.
32 devices in a mesh: groups: 2 (over y), seq: 4 (over z), chan: 2 (over x), rep: 2 (over core).
Axes of the slice: x: 2, y: 2, z: 4, core: 2. Of those that a mesh axis runs over, the one named last changes fastest.
Arguments:
- query_proj: bfloat16 [2048, 8192], P(('groups', 'seq'), ('chan', 'rep')), parts along dimension 0, may hold values from -6 to 6
- key_proj: bfloat16 [2048, 8192], P(('groups', 'seq'), ('chan', 'rep')), parts along dimension 0, may hold values from -6 to 6
- value_proj: bfloat16 [2048, 8192], P(('groups', 'seq'), ('chan', 'rep')), parts along dimension 0, may hold values from -6 to 6
- short_taps: bfloat16 [7, 8192], P(None, ('chan', 'rep')), may hold values from -2 to 2
- medium_taps: bfloat16 [128, 512], P(None, ('chan', 'rep')), may hold values from -0.5 to 0.5
- modal_poles: float32 [4, 512, 16], P(None, ('chan', 'rep')), may hold values from -3.1416 to 3.1416, as said below
- skip_gain: float32 [8192], P(('chan', 'rep')), may hold values from 0.5 to 1.5
- norm_gain: float32 [8192], P(('chan', 'rep')), may hold values from 0.5 to 1.5
- unembed: bfloat16 [8192, 512], P(('chan', 'rep')), may hold values from -0.1875 to 0.1875
- token_ids: int32 [2048], P(('groups', 'seq')), parts along dimension 0, may hold values from 0 to 511
- genome_lengths: int32 [16], P('groups'), parts along dimension 0, may hold values from 1 to 512, 1024 in all
Outputs:
- token_logprob: float32 [2048], P(('groups', 'seq')), parts along dimension 0
- genome_score: float32 [16], P('groups'), parts along dimension 0
There are 2 independent parts, one for each index of `groups`. A program takes and returns all parts, laid end to end along the dimension named above; an argument that names none is the same for every part. Nothing has to cross between parts.
Inputs may be any that keep to these rules, and one draw needn't show every extreme that they name: `genome_lengths`: the 8 genomes are packed end to end from position 0; their lengths sum to 1024. `modal_poles`: row 0 holds positive decay rates, row 1 angles, rows 2 and 3 residues.
All inputs are finite; a program needn't handle non-finite values.
Results may differ from a plain program's by a relative error of at most 0.0033.
Values may be sent and summed in bfloat16 or wider, within the bound.
No kernel may reach another device: no remote copies, remote signals or barrier semaphores. Data moves between devices by JAX's collectives and lax.ppermute only.
A program may use at most 128 MiB of HBM per device.

v0:
```python
import jax
import jax.numpy as jnp
from jax import lax
from jax.sharding import PartitionSpec as P

D = 8192
GROUP = 16
tile_rows = 128
short_margin = 8
norm_eps = 1e-05


def from_behind(shard, axis, by):
    count = lax.axis_size(axis)
    pairs = [(i, i + by) for i in range(count) if 0 <= i + by < count]
    return lax.ppermute(shard, axis, pairs)


def entering_2(part, axis, combine, identity):
    place = lax.axis_index(axis)
    gathered = jax.tree.map(lambda a: lax.all_gather(a, axis), part)
    state = jax.tree.map(lambda a, e: jnp.zeros_like(a) + jnp.asarray(e, a.dtype), part, identity)

    def one(step, state):
        return combine(
            state, jax.tree.map(lambda a: lax.dynamic_index_in_dim(a, step, 0, False), gathered)
        )

    return lax.fori_loop(0, place, one, state)


def segment_ids(positions, genome_lengths):
    starts = jnp.cumsum(genome_lengths) - genome_lengths
    at_or_past = (positions[:, None] >= starts[None, :]).astype(jnp.int32)
    return jnp.sum(at_or_past, axis=1) - 1


def short_filter(keys_in, values_in, seg_list, out_rows, short_taps):
    gated = keys_in.astype(jnp.float32) * values_in.astype(jnp.float32)
    total_rows = keys_in.shape[0]
    lead_rows = total_rows - out_rows
    own_segs = seg_list[lead_rows:]
    result = jnp.zeros((out_rows, keys_in.shape[1]), jnp.float32)
    for lag_index in range(short_taps.shape[0]):
        shifted = gated[lead_rows - lag_index : total_rows - lag_index]
        same_genome = (seg_list[lead_rows - lag_index : total_rows - lag_index] == own_segs).astype(
            jnp.float32
        )
        result = (
            result
            + short_taps[lag_index].astype(jnp.float32)[None, :] * shifted * same_genome[:, None]
        )
    return result.astype(jnp.bfloat16)


def medium_toeplitz(medium_taps):
    out_pos = jnp.arange(tile_rows, dtype=jnp.int32)[:, None]
    in_pos = jnp.arange(2 * tile_rows, dtype=jnp.int32)[None, :]
    lag_grid = out_pos + tile_rows - in_pos
    tap_count = medium_taps.shape[0]
    valid = (lag_grid >= 0) & (lag_grid < tap_count)
    gathered = jnp.take(medium_taps, jnp.clip(lag_grid, 0, tap_count - 1), axis=0)
    masked = jnp.where(valid[:, :, None], gathered, jnp.zeros_like(gathered))
    return jnp.transpose(masked, (2, 0, 1))


def modal_tables(modal_poles):
    decay_rate = modal_poles[0]
    angles = modal_poles[1]
    residue_re = modal_poles[2]
    residue_im = modal_poles[3]
    powers = jnp.arange(tile_rows + 1).astype(jnp.float32)[:, None, None]
    magnitude = jnp.exp(-powers * decay_rate[None])
    power_re = magnitude * jnp.cos(powers * angles[None])
    power_im = magnitude * jnp.sin(powers * angles[None])
    kernel_re = residue_re[None] * power_re - residue_im[None] * power_im
    kernel_im = residue_re[None] * power_im + residue_im[None] * power_re
    kernel = jnp.sum(kernel_re[:tile_rows], axis=2)
    lag_grid = (
        jnp.arange(tile_rows, dtype=jnp.int32)[:, None]
        - jnp.arange(tile_rows, dtype=jnp.int32)[None, :]
    )
    taken = jnp.take(kernel, jnp.clip(lag_grid, 0, tile_rows - 1), axis=0)
    toeplitz = jnp.transpose(
        jnp.where((lag_grid >= 0)[:, :, None], taken, jnp.zeros_like(taken)), (2, 0, 1)
    )
    outward = jnp.transpose(jnp.concatenate((kernel_re[1:], -kernel_im[1:]), axis=2), (1, 0, 2))
    inward = jnp.transpose(
        jnp.concatenate((power_re[tile_rows - 1 :: -1], power_im[tile_rows - 1 :: -1]), axis=2),
        (1, 0, 2),
    )
    return (toeplitz, outward, inward, power_re[tile_rows], power_im[tile_rows])


def split_table(table):
    upper = table.astype(jnp.bfloat16)
    lower = (table - upper.astype(jnp.float32)).astype(jnp.bfloat16)
    return (upper, lower)


def complex_link(earlier, later):
    early_are, early_aim, early_sre, early_sim = earlier
    late_are, late_aim, late_sre, late_sim = later
    lead_re = late_are[..., None, :]
    lead_im = late_aim[..., None, :]
    return (
        late_are * early_are - late_aim * early_aim,
        late_are * early_aim + late_aim * early_are,
        lead_re * early_sre - lead_im * early_sim + late_sre,
        lead_re * early_sim + lead_im * early_sre + late_sim,
    )


def log_probs(logits, targets):
    vocab_ids = jnp.arange(logits.shape[1], dtype=jnp.int32)
    picked = jnp.sum(
        jnp.where(targets[:, None] == vocab_ids[None, :], logits, jnp.zeros_like(logits)), axis=1
    )
    return picked - jnp.log(jnp.sum(jnp.exp(logits), axis=1))


def channel_logits(normed_cols, unembed):
    return lax.dot_general(
        normed_cols, unembed, (((0,), (0,)), ((), ())), preferred_element_type=jnp.float32
    )


def per_device(
    query_proj,
    key_proj,
    value_proj,
    short_taps,
    medium_taps,
    modal_poles,
    skip_gain,
    norm_gain,
    unembed,
    token_ids,
    genome_lengths,
):
    highest = lax.Precision.HIGHEST
    row_count, chan_count = query_proj.shape
    group_count = chan_count // GROUP
    mode_count = modal_poles.shape[2]
    tile_count = row_count // tile_rows
    first_row = lax.axis_index("seq") * row_count
    segments = segment_ids(first_row + jnp.arange(row_count, dtype=jnp.int32), genome_lengths)
    edge_pair = from_behind(
        jnp.stack((key_proj[row_count - short_margin :], value_proj[row_count - short_margin :])),
        "seq",
        1,
    )
    ext_segs = segment_ids(
        first_row - short_margin + jnp.arange(row_count + short_margin, dtype=jnp.int32),
        genome_lengths,
    )
    filtered = short_filter(
        jnp.concatenate((edge_pair[0], key_proj)),
        jnp.concatenate((edge_pair[1], value_proj)),
        ext_segs,
        row_count,
        short_taps,
    )
    previous = from_behind(filtered[row_count - tile_rows :], "seq", 1)
    ext_short = jnp.concatenate((previous, filtered)).T.reshape(
        group_count, GROUP, row_count + tile_rows
    )
    medium_segs = segment_ids(
        first_row - tile_rows + jnp.arange(row_count + tile_rows, dtype=jnp.int32), genome_lengths
    )
    toeplitz = medium_toeplitz(medium_taps)

    def medium_block(tile_index):
        start = tile_index * tile_rows
        window = lax.dynamic_slice_in_dim(ext_short, start, 2 * tile_rows, 2)
        window_segs = lax.dynamic_slice_in_dim(medium_segs, start, 2 * tile_rows, 0)
        own_segs = lax.dynamic_slice_in_dim(segments, start, tile_rows, 0)
        same_genome = own_segs[:, None] == window_segs[None, :]
        matrix = jnp.where(same_genome[None], toeplitz, jnp.zeros_like(toeplitz))
        return jnp.einsum(
            "gts,gis->git", matrix, window, preferred_element_type=jnp.float32
        ).astype(jnp.bfloat16)

    signal = lax.map(medium_block, jnp.arange(tile_count, dtype=jnp.int32))
    long_toeplitz, outward, inward, decay_re, decay_im = modal_tables(modal_poles)
    toeplitz_upper, toeplitz_lower = split_table(long_toeplitz)
    inward_upper, inward_lower = split_table(inward)
    tile_segs = segments.reshape(tile_count, tile_rows)
    before = segment_ids(
        first_row + jnp.arange(tile_count, dtype=jnp.int32) * tile_rows - 1, genome_lengths
    )

    def intra_block(inputs):
        block_in, own_segs = inputs
        same_genome = (own_segs[:, None] == own_segs[None, :])[None]
        upper = jnp.where(same_genome, toeplitz_upper, jnp.zeros_like(toeplitz_upper))
        lower = jnp.where(same_genome, toeplitz_lower, jnp.zeros_like(toeplitz_lower))
        return jnp.einsum(
            "gts,gis->git", upper, block_in, preferred_element_type=jnp.float32
        ) + jnp.einsum("gts,gis->git", lower, block_in, preferred_element_type=jnp.float32)

    local_part = lax.map(intra_block, (signal, tile_segs))
    end_keep = (tile_segs == tile_segs[:, -1:])[:, None, None, :]
    masked_signal = jnp.where(end_keep, signal, jnp.zeros_like(signal))
    states = jnp.einsum(
        "gsm,jgis->jgim", inward_upper, masked_signal, preferred_element_type=jnp.float32
    ) + jnp.einsum(
        "gsm,jgis->jgim", inward_lower, masked_signal, preferred_element_type=jnp.float32
    )
    carried = (tile_segs[:, -1] == before).astype(jnp.float32)

    def chain_link(carry_in, inputs):
        block_states, kept_flag = inputs
        step = (
            decay_re * kept_flag,
            decay_im * kept_flag,
            block_states[..., :mode_count],
            block_states[..., mode_count:],
        )
        return (complex_link(carry_in, step), carry_in)

    state_zero = jnp.zeros((group_count, GROUP, mode_count), jnp.float32)
    start_carry = (
        jnp.ones((group_count, mode_count), jnp.float32),
        jnp.zeros((group_count, mode_count), jnp.float32),
        state_zero,
        state_zero,
    )
    summary, entering = lax.scan(chain_link, start_carry, (states, carried))
    incoming = entering_2(
        (summary[0], summary[1], summary[2], summary[3]),
        "seq",
        complex_link,
        (start_carry[0], start_carry[1], start_carry[2], start_carry[3]),
    )
    incoming_re = incoming[2]
    incoming_im = incoming[3]
    reach_re = entering[0][:, :, None, :]
    reach_im = entering[1][:, :, None, :]
    full_re = entering[2] + reach_re * incoming_re - reach_im * incoming_im
    full_im = entering[3] + reach_re * incoming_im + reach_im * incoming_re
    keep_mask = (tile_segs == before[:, None]).astype(jnp.float32)
    carried_part = (
        jnp.einsum(
            "gtm,jgim->jgit",
            outward,
            jnp.concatenate((full_re, full_im), axis=3),
            precision=highest,
        )
        * keep_mask[:, None, None, :]
    )
    longconv = (
        local_part
        + carried_part
        + skip_gain.reshape(group_count, GROUP)[None, :, :, None] * signal.astype(jnp.float32)
    )
    long_cols = jnp.transpose(longconv, (1, 2, 0, 3)).reshape(chan_count, row_count)
    mixed = (query_proj.T.astype(jnp.float32) * long_cols).astype(jnp.bfloat16)
    mixed_wide = mixed.astype(jnp.float32)
    squares = lax.psum(jnp.sum(mixed_wide * mixed_wide, axis=0), ("chan", "rep"))
    normed = (mixed_wide * lax.rsqrt(squares / D + norm_eps)[None, :] * norm_gain[:, None]).astype(
        jnp.bfloat16
    )
    partial_value = channel_logits(normed, unembed)
    logits = lax.psum(partial_value, ("chan", "rep"))
    logprob = log_probs(logits, token_ids)
    genome_index = jnp.arange(genome_lengths.shape[0], dtype=jnp.int32)
    genome_part = jnp.sum(
        jnp.where(
            segments[:, None] == genome_index[None, :],
            logprob[:, None],
            jnp.zeros((row_count, genome_lengths.shape[0]), jnp.float32),
        ),
        axis=0,
    )
    totals = lax.psum(genome_part, "seq")
    return (logprob, totals / genome_lengths.astype(jnp.float32))


def solution(mesh):
    return jax.shard_map(
        per_device,
        mesh=mesh,
        in_specs=(
            P(("groups", "seq"), ("chan", "rep")),
            P(("groups", "seq"), ("chan", "rep")),
            P(("groups", "seq"), ("chan", "rep")),
            P(None, ("chan", "rep")),
            P(None, ("chan", "rep")),
            P(None, ("chan", "rep"), None),
            P(("chan", "rep")),
            P(("chan", "rep")),
            P(("chan", "rep"), None),
            P(("groups", "seq")),
            P("groups"),
        ),
        out_specs=(P(("groups", "seq")), P("groups")),
        check_vma=False,
    )
```

profile of v0, /device:TPU:0, one launch (start us, length us, event | category | flops | bytes accessed | tf_op | source)
XLA Modules:
  0.0 474.0 jit_solution(14729307594950726324)
XLA Ops:
  8.8 5.5 %collective-permute-start = (bf16[2,8,2048]{2,1,0:T(8,128)(2,1)}, bf16[2,8,2048]{2,1,0:T(8,128)(2,1)}, u32[]{:S(2)}, u32[]{:S(2)}) collective-permute-start(bf16[2,8,2048]{2,1,0:T(8,128)(2,1)} %pad_maximum_fusion.1), channel_id=1, source_target_pairs={{0,4},{4,8},{8,12},{1,5},{5,9},{9,13},{2,6},{6,10},{10,14},{3,7},{... | collective-permute-start | bytes 196616 | tf_op jit(solution)/shard_map/ppermute | solution.py:16
  20.1 114.1 %gather_fusion = bf16[32768,128]{1,0:T(8,128)(2,1)} fusion(bf16[128,128]{1,0:T(8,128)(2,1)S(1)} %copy-done.1, s32[32768]{0:T(1024)S(1)} %broadcast_clamp_fusion), kind=kCustom, calls=%fused_computation | custom fusion | bytes 16908288 | tf_op jit(solution)/shard_map/jit(_take)/gather | solution.py:62
  134.3 12.9 %copy.87 = bf16[128,256,128]{1,0,2:T(8,128)(2,1)} copy(bf16[128,256,128]{2,1,0:T(8,128)(2,1)} %bitcast.210) | data formatting | bytes 16777216 | tf_op jit(solution)/shard_map/jit(_take)/gather | solution.py:62
  147.9 9.5 %fusion.47 = (f32[129,128,16]{0,2,1:T(8,128)}, f32[129,128,16]{0,2,1:T(8,128)S(1)}, f32[129,128,16]{0,2,1:T(8,128)}) fusion(f32[128,16]{1,0:T(8,128)S(1)} %copy.90, f32[129]{0:T(256)S(1)} %iota_convert_fusion, f32[128,16]{1,0:T(8,128)S(1)} %copy.89, f32[129]{0:T(256)S(1)} %fusion.95, f32[128,16]{1,0:T(8,128)S(1)} %copy.91, f32[128,16]{1,0:T(8,128)S(1)} %copy.88), kind=kLoop, calls=%fused_computation.66 | loop fusion | flops 1849344 | bytes 3204104 | tf_op jit(solution)/shard_map/mul | solution.py:75
  158.9 54.5 %gather_fusion.1 = f32[16384,128]{1,0:T(8,128)} fusion(f32[128,128]{1,0:T(8,128)S(1)} %copy.92, s32[16384]{0:T(1024)S(1)} %fusion.89), kind=kCustom, calls=%fused_computation.1 | custom fusion | bytes 16842752 | tf_op jit(solution)/shard_map/jit(_take)/gather | solution.py:83
  213.4 9.3 %copy.93 = f32[128,128,128]{1,0,2:T(8,128)} copy(f32[128,128,128]{2,1,0:T(8,128)} %bitcast.211) | data formatting | bytes 16777216 | tf_op jit(solution)/shard_map/jit(_take)/gather | solution.py:83
  227.9 7.5 %select_bitcast_fusion = bf16[128,128,256]{2,1,0:T(8,128)(2,1)} fusion(bf16[128,256,128]{1,0,2:T(8,128)(2,1)} %copy.87, pred[128,256]{1,0:T(8,128)(4,1)S(1)} %get-tuple-element.472, pred[128,256]{1,0:T(8,128)(4,1)S(1)} %get-tuple-element.471), kind=kLoop, calls=%fused_computation.56 | loop fusion | flops 8388608 | bytes 16842752 | tf_op jit(solution)/shard_map/jit(_where)/select_n | solution.py:63
  235.4 6.8 %fusion.42 = bf16[128,128,128]{2,1,0:T(8,128)(2,1)} fusion(f32[128,128,128]{1,0,2:T(8,128)} %copy.93, pred[128,128]{1,0:T(8,128)(4,1)S(1)} %get-tuple-element.476, pred[128,128]{1,0:T(8,128)(4,1)S(1)} %get-tuple-element.475), kind=kLoop, calls=%fused_computation.54 | loop fusion | flops 12582912 | bytes 12615680 | tf_op jit(solution)/shard_map/convert_element_type | solution.py:97
  269.7 7.3 %collective-permute-done.1 = bf16[128,2048]{1,0:T(8,128)(2,1)S(1)} collective-permute-done((bf16[128,2048]{1,0:T(8,128)(2,1)S(1)}, bf16[128,2048]{1,0:T(8,128)(2,1)S(1)}, u32[]{:S(2)}, u32[]{:S(2)}) %collective-permute-start.1) | collective-permute-done | bytes 524320 | tf_op jit(solution)/shard_map/ppermute | solution.py:16
  280.9 15.2 %while.64 = (s32[]{:T(128)}, bf16[2,128,16,128]{3,2,1,0:T(8,128)(2,1)S(1)}, s32[2]{0:T(128)S(1)}, bf16[128,16,384]{2,1,0:T(8,128)(2,1)}, s32[256]{0:T(256)S(1)},...) while((s32[]{:T(128)}, bf16[2,128,16,128]{3,2,1,0:T(8,128)(2,1)S(1)}, ...), condition=%wide.region_5.6_spmd.clone, body=%wide.region_4.5_spmd.sunk.clone | while | flops 138706944 | bytes 10032308 | solution.py:184
  282.4 6.1 %fusion.126 = bf16[2,128,16,128]{3,2,1,0:T(8,128)(2,1)S(1)} fusion(bf16[2,128,16,128]{3,2,1,0:T(8,128)(2,1)S(1)} %get-tuple-element.826, s32[]{:T(128)} %get-tuple-element.825, bf16[128,128,256]{2,1,0:T(8,128)(2,1)} %get-tuple-element.839, pred[128,256]{1,0:T(8,128)(4,1)S(1)} %broadcast_compare_fusion.7, ...), kind=kOutput, calls=%fused_computation.8.clone.1.clone | convolution fusion | flops 138674176 | bytes 9994756 | tf_op jit(solution)/shard_map/while/body/eval_jaxpr/gts,gis->git/dot_general | solution.py:180
  290.0 6.1 %fusion.126 = bf16[2,128,16,128]{3,2,1,0:T(8,128)(2,1)S(1)} fusion(bf16[2,128,16,128]{3,2,1,0:T(8,128)(2,1)S(1)} %get-tuple-element.826, s32[]{:T(128)} %get-tuple-element.825, bf16[128,128,256]{2,1,0:T(8,128)(2,1)} %get-tuple-element.839, pred[128,256]{1,0:T(8,128)(4,1)S(1)} %broadcast_compare_fusion.7, ...), kind=kOutput, calls=%fused_computation.8.clone.1.clone | convolution fusion | flops 138674176 | bytes 9994756 | tf_op jit(solution)/shard_map/while/body/eval_jaxpr/gts,gis->git/dot_general | solution.py:180
  304.0 7.3 %while.67 = (s32[]{:T(128)}, f32[128,16]{0,1:T(8,128)S(1)}, f32[128,16]{0,1:T(8,128)S(1)}, f32[128,16,16]{0,2,1:T(8,128)S(1)}, f32[128,16,16]{0,2,1:T(8,128)S(1)...) while((s32[]{:T(128)}, f32[128,16]{0,1:T(8,128)S(1)}, ...), condition=%wide.region_11.12_spmd.clone.clone, body=%wide.region_10.11_spmd.clone.sunk.clone | while | flops 421891 | bytes 2000031 | solution.py:229
  311.3 17.7 %all-gather.2 = f32[512,16,16]{0,2,1:T(8,128)} all-gather(f32[128,16,16]{0,2,1:T(8,128)S(1)} %get-tuple-element.221), channel_id=4, replica_groups=mesh['groups'=2,'seq'=4,'chan'=2,'rep'=2] {'seq'}, dimensions={0}, use_global_device_ids=true | all-gather | bytes 655360 | tf_op jit(solution)/shard_map/all_gather | solution.py:21
  331.1 15.5 %all-gather.3 = f32[512,16,16]{0,2,1:T(8,128)} all-gather(f32[128,16,16]{0,2,1:T(8,128)S(1)} %get-tuple-element.222), channel_id=5, replica_groups=mesh['groups'=2,'seq'=4,'chan'=2,'rep'=2] {'seq'}, dimensions={0}, use_global_device_ids=true | all-gather | bytes 655360 | tf_op jit(solution)/shard_map/all_gather | solution.py:21
  348.6 13.1 %all-gather = f32[512,16]{0,1:T(8,128)S(1)} all-gather(f32[128,16]{0,1:T(8,128)S(1)} %get-tuple-element.219), channel_id=2, replica_groups=mesh['groups'=2,'seq'=4,'chan'=2,'rep'=2] {'seq'}, dimensions={0}, use_global_device_ids=true | all-gather | bytes 40960 | tf_op jit(solution)/shard_map/all_gather | solution.py:21
  361.7 13.1 %all-gather.1 = f32[512,16]{0,1:T(8,128)S(1)} all-gather(f32[128,16]{0,1:T(8,128)S(1)} %get-tuple-element.220), channel_id=3, replica_groups=mesh['groups'=2,'seq'=4,'chan'=2,'rep'=2] {'seq'}, dimensions={0}, use_global_device_ids=true | all-gather | bytes 40960 | tf_op jit(solution)/shard_map/all_gather | solution.py:21
  381.0 16.2 %while.65 = (s32[]{:T(128)}, f32[2,128,16,128]{3,2,0,1:T(8,128)}, bf16[2,128,16,128]{3,2,1,0:T(8,128)(2,1)S(1)}, s32[2,128]{1,0:T(2,128)S(1)}, bf16[128,128,128]{2,1,0:T(8,128)(2,1)}, /*index=5*/bf16[128,128,128]{2,1,0:T(8,128)(2,1)}) while((s32[]{:T(128)}, f32[2,128,16,128]{3,2,0,1:T(8,128)}, ...), condition=%wide.region_8.9_spmd.clone, body=%wide.region_7.8_spmd.sunk.clone | while | flops 138690560 | bytes 29411944 | solution.py:202
  381.2 4.6 fusion.132
  389.3 4.6 fusion.132
  397.3 5.3 %fusion.66 = f32[128,16,2,128]{3,1,2,0:T(8,128)S(1)} fusion(f32[2,128,16,128]{3,2,0,1:T(8,128)} %get-tuple-element.216, f32[2,128,16,32]{3,2,0,1:T(8,128)} %copy.103, f32[128,128,16]{0,2,1:T(8,128)} %get-tuple-element.440, f32[128,128,16]{0,2,1:T(8,128)} %get-tuple-element.438, bf16[2,128,16,128]{3,2,1,0:T(8,128)(2,1)S(1)} %get-tuple-element.923, ...), kind=kOutput, calls=%fused_computation.96 | convolution fusion | flops 204472320 | bytes 7873536 | tf_op jit(solution)/shard_map/gtm,jgim->jgit/dot_general | solution.py:244
  405.4 5.7 %psum.21 = f32[256]{0:T(256)S(1)} all-reduce(f32[256]{0:T(256)S(1)} %fusion.43), channel_id=1, replica_groups=mesh['groups'=2,'seq'=4,'chan'=2,'rep'=2] {'chan','rep'}, use_global_device_ids=true, to_apply=%region_15.16 | all-reduce | flops 256 | bytes 2048 | tf_op jit(solution)/shard_map/psum | solution.py:260
  414.9 38.6 %all-reduce.2.cloned.1.call-done = f32[256,512]{1,0:T(8,128)} async-done(((f32[256,512]{1,0:T(8,128)}), f32[256,512]{1,0:T(8,128)}) %all-reduce.2.cloned.1.call-update) | async-done | bytes 524304 | tf_op jit(solution)/shard_map/psum | solution.py:265
  454.9 11.7 %psum.23 = f32[8]{0:T(128)S(1)} all-reduce(f32[8]{0:T(128)S(1)} %select_reduce_fusion.1), channel_id=1, replica_groups=mesh['groups'=2,'seq'=4,'chan'=2,'rep'=2] {'seq'}, use_global_device_ids=true, to_apply=%region_20.21 | all-reduce | flops 8 | bytes 64 | tf_op jit(solution)/shard_map/psum | solution.py:276
  (192 shorter events, 88.5 us)
Async XLA Ops:
  7.2 403.9 %copy-start = (bf16[2048,512]{1,0:T(8,128)(2,1)S(1)}, bf16[2048,512]{1,0:T(8,128)(2,1)}, u32[]{:S(2)}) copy-start(bf16[2048,512]{1,0:T(8,128)(2,1)} %param.27) | copy-start | bytes 6291460
  7.2 13.0 %copy-start.1 = (bf16[128,128]{1,0:T(8,128)(2,1)S(1)}, bf16[128,128]{1,0:T(8,128)(2,1)}, u32[]{:S(2)}) copy-start(bf16[128,128]{1,0:T(8,128)(2,1)} %param.23) | copy-start | bytes 98308
  7.2 446.3 %all-reduce.2.cloned.1.call-start = ((), (), s32[]{:S(2)}) async-start(), calls=%async_computation | async-start | bytes 1048576 | tf_op jit(solution)/shard_map/psum | solution.py:265
  8.8 248.4 %collective-permute-start = (bf16[2,8,2048]{2,1,0:T(8,128)(2,1)}, bf16[2,8,2048]{2,1,0:T(8,128)(2,1)}, u32[]{:S(2)}, u32[]{:S(2)}) collective-permute-start(bf16[2,8,2048]{2,1,0:T(8,128)(2,1)} %pad_maximum_fusion.1), channel_id=1, source_target_pairs={{0,4},{4,8},{8,12},{1,5},{5,9},{9,13},{2,6},{6,10},{10,14},{3,7},{... | collective-permute-start | bytes 196616 | tf_op jit(solution)/shard_map/ppermute | solution.py:16
  19.4 128.2 %copy-start.28 = (s32[2,128]{1,0:T(2,128)}, s32[2,128]{1,0:T(2,128)S(1)}, u32[]{:S(2)}) copy-start(s32[2,128]{1,0:T(2,128)S(1)} %get-tuple-element.844) | copy-start | bytes 3076
  134.3 12.9 %copy-start.13 = (f32[4,128,16]{1,2,0:T(8,128)S(1)}, f32[4,128,16]{1,2,0:T(8,128)}, u32[]{:S(2)}) copy-start(f32[4,128,16]{1,2,0:T(8,128)} %param.24) | copy-start | bytes 98308
  242.7 2.4 copy-start.2
  260.0 6.3 %slice-start = ((s8[8388608]{0:T(1024)(128)(4,1)}), s8[4194304]{0:T(1024)(128)(4,1)S(1)}, s32[]{:S(2)}) async-start(s8[8388608]{0:T(1024)(128)(4,1)} %bitcast.208), calls=%async_computation.1 | async-start | bytes 8388608
  260.1 6.2 %slice-start.1 = ((s8[8388608]{0:T(1024)(128)(4,1)}), s8[4194304]{0:T(1024)(128)(4,1)S(1)}, s32[]{:S(2)}) async-start(s8[8388608]{0:T(1024)(128)(4,1)} %bitcast.208), calls=%async_computation.2 | async-start | bytes 8388608
  263.2 13.8 %collective-permute-start.1 = (bf16[128,2048]{1,0:T(8,128)(2,1)S(1)}, bf16[128,2048]{1,0:T(8,128)(2,1)S(1)}, u32[]{:S(2)}, u32[]{:S(2)}) collective-permute-start(bf16[128,2048]{1,0:T(8,128)(2,1)S(1)} %slice.177), channel_id=1, source_target_pairs={{0,4},{4,8},{8,12},{1,5},{5,9},{9,13},{2,6},{6,10},{10,14},{3,7},{... | collective-permute-start | bytes 1572872 | tf_op jit(solution)/shard_map/ppermute | solution.py:16
  278.2 2.6 copy-start.14
  278.2 2.6 copy-start.24
  280.9 15.2 %copy-start.16 = (pred[2,128]{1,0:T(4,128)(4,1)S(1)}, pred[2,128]{1,0:T(4,128)(4,1)}, u32[]{:S(2)}) copy-start(pred[2,128]{1,0:T(4,128)(4,1)} %get-tuple-element.468) | copy-start | bytes 772
  300.5 3.5 copy-start.15
  300.5 3.5 copy-start.32
  376.2 4.8 %copy-start.29 = (s32[2,128]{1,0:T(2,128)S(1)}, s32[2,128]{1,0:T(2,128)}, u32[]{:S(2)}) copy-start(s32[2,128]{1,0:T(2,128)} %copy-done.28) | copy-start | bytes 3076
  381.0 16.2 %copy-start.17 = (f32[2,128]{1,0:T(2,128)S(1)}, f32[2,128]{1,0:T(2,128)}, u32[]{:S(2)}) copy-start(f32[2,128]{1,0:T(2,128)} %get-tuple-element.467) | copy-start | bytes 3076
  381.1 4.6 copy-start.6
  389.3 4.6 copy-start.6
  403.7 7.3 %copy-start.30 = (f32[2048]{0:T(1024)S(1)}, f32[2048]{0:T(1024)}, u32[]{:S(2)}) copy-start(f32[2048]{0:T(1024)} %param.26) | copy-start | bytes 24580
  411.1 42.5 %copy-start.27 = (s32[256]{0:T(256)S(1)}, s32[256]{0:T(256)}, u32[]{:S(2)}) copy-start(s32[256]{0:T(256)} %param.28) | copy-start | bytes 3076
  411.1 43.7 %copy-start.25 = (s32[256]{0:T(256)S(1)}, s32[256]{0:T(256)}, u32[]{:S(2)}) copy-start(s32[256]{0:T(256)} %get-tuple-element.821) | copy-start | bytes 3076
  411.1 55.5 %copy-start.31 = (s32[8]{0:T(128)S(1)}, s32[8]{0:T(128)}, u32[]{:S(2)}) copy-start(s32[8]{0:T(128)} %param.29) | copy-start | bytes 100
  454.8 12.3 %copy-start.26 = (f32[256]{0:T(256)}, f32[256]{0:T(256)S(1)}, u32[]{:S(2)}) copy-start(f32[256]{0:T(256)S(1)} %log_subtract_fusion) | copy-start | bytes 3076
  (15 other events, 31.2 us)
Sparse Core Ops, SparseCore 0:
  415.1 38.4 all-reduce.1
where the time goes:
time: 476 us; the launch traced here: 474 us
  local copies, waits for them, and re-layouts  229 us (48%)
  blocking collectives  76.8 us (16%)
  other arithmetic  55.6 us (12%)
  waiting for transfers between devices  45.9 us (10%)
  matrix products  41.7 us (9%)
  between operations  14.6 us (3%)
  starting transfers between devices  8.67 us (2%)
    gather x2, local copies, waits for them, and re-layouts, medium_toeplitz(): jnp.take(medium_taps, jnp.clip(lag_grid, 0, tap_count - 1), axis=0)  127 us
    gather x2, local copies, waits for them, and re-layouts, modal_tables(): taken = jnp.take(kernel, jnp.clip(lag_grid, 0, tile_rows - 1), axis=0)  63.8 us
    all_gather x4, blocking collectives, entering_2(): gathered = jax.tree.map(lambda a: lax.all_gather(a, axis), part)  59.4 us
    psum x1, waiting for transfers between devices, per_device(): logits = lax.psum(partial_value, ('chan', 'rep'))  38.6 us
    dot_general x2, matrix products, medium_block(): jnp.einsum('gts,gis->git', matrix, window, preferred_element_type=jnp.flo...  12.2 us
    psum x1, blocking collectives, per_device(): totals = lax.psum(genome_part, 'seq')  11.7 us
  transfers between devices with their start and end apart: 3, of which 2 were waited for; matrix products, arithmetic and copies ran while one was open for 52% of the time, Pallas kernels for 0%

commit v1 on v0

--- a/solution.py
+++ b/solution.py
@@ -262,7 +262,8 @@
         jnp.bfloat16
     )
     partial_value = channel_logits(normed, unembed)
-    logits = lax.psum(partial_value, ("chan", "rep"))
+    one_axis = lax.psum(partial_value, "rep")
+    logits = lax.psum(one_axis, "chan")
     logprob = log_probs(logits, token_ids)
     genome_index = jnp.arange(genome_lengths.shape[0], dtype=jnp.int32)
     genome_part = jnp.sum(

time: 476 us -> 493 us (1.036)
  waiting for transfers between devices: 45.9 us -> 63.6 us
    psum x1 -> x2, waiting for transfers between devices: 38.6 us -> 56.3 us  [the longest x1 32.2 us: per_device(): logits = lax.psum(one_axis, 'chan')]
  transfers between devices with their start and end apart: 3 -> 4, of which waited for: 2 -> 3; matrix products, arithmetic and copies ran while one was open for 52% -> 50% of each run, Pallas kernels for 0% -> 0%
where the time goes in v1:
time: 493 us; the launch traced here: 492 us
  local copies, waits for them, and re-layouts  229 us (46%)
  blocking collectives  76.8 us (16%)
  waiting for transfers between devices  63.6 us (13%)
  other arithmetic  55.6 us (11%)
  matrix products  41.7 us (8%)
  between operations  14.6 us (3%)
  starting transfers between devices  8.71 us (2%)
    gather x2, local copies, waits for them, and re-layouts, medium_toeplitz(): jnp.take(medium_taps, jnp.clip(lag_grid, 0, tap_count - 1), axis=0)  127 us
    gather x2, local copies, waits for them, and re-layouts, modal_tables(): taken = jnp.take(kernel, jnp.clip(lag_grid, 0, tile_rows - 1), axis=0)  63.8 us
    all_gather x4, blocking collectives, entering_2(): gathered = jax.tree.map(lambda a: lax.all_gather(a, axis), part)  59.4 us
    psum x1, waiting for transfers between devices, per_device(): logits = lax.psum(one_axis, 'chan')  32.2 us
    psum x1, waiting for transfers between devices, per_device(): one_axis = lax.psum(partial_value, 'rep')  24.1 us
    dot_general x2, matrix products, medium_block(): jnp.einsum('gts,gis->git', matrix, window, preferred_element_type=jnp.flo...  12.2 us
    psum x1, blocking collectives, per_device(): totals = lax.psum(genome_part, 'seq')  11.7 us
  transfers between devices with their start and end apart: 4, of which 3 were waited for; matrix products, arithmetic and copies ran while one was open for 50% of the time, Pallas kernels for 0%

profile of v1, /device:TPU:0, one launch (start us, length us, event | category | flops | bytes accessed | tf_op | source)
XLA Modules:
  0.0 491.8 jit_solution(15063124474667674553)
XLA Ops:
  8.8 5.5 %collective-permute-start = (bf16[2,8,2048]{2,1,0:T(8,128)(2,1)}, bf16[2,8,2048]{2,1,0:T(8,128)(2,1)}, u32[]{:S(2)}, u32[]{:S(2)}) collective-permute-start(bf16[2,8,2048]{2,1,0:T(8,128)(2,1)} %pad_maximum_fusion.1), channel_id=1, source_target_pairs={{0,4},{4,8},{8,12},{1,5},{5,9},{9,13},{2,6},{6,10},{10,14},{3,7},{... | collective-permute-start | bytes 196616 | tf_op jit(solution)/shard_map/ppermute | solution.py:16
  20.1 114.1 %gather_fusion = bf16[32768,128]{1,0:T(8,128)(2,1)} fusion(bf16[128,128]{1,0:T(8,128)(2,1)S(1)} %copy-done.1, s32[32768]{0:T(1024)S(1)} %broadcast_clamp_fusion), kind=kCustom, calls=%fused_computation | custom fusion | bytes 16908288 | tf_op jit(solution)/shard_map/jit(_take)/gather | solution.py:62
  134.3 12.9 %copy.87 = bf16[128,256,128]{1,0,2:T(8,128)(2,1)} copy(bf16[128,256,128]{2,1,0:T(8,128)(2,1)} %bitcast.210) | data formatting | bytes 16777216 | tf_op jit(solution)/shard_map/jit(_take)/gather | solution.py:62
  147.9 9.5 %fusion.47 = (f32[129,128,16]{0,2,1:T(8,128)}, f32[129,128,16]{0,2,1:T(8,128)S(1)}, f32[129,128,16]{0,2,1:T(8,128)}) fusion(f32[128,16]{1,0:T(8,128)S(1)} %copy.90, f32[129]{0:T(256)S(1)} %iota_convert_fusion, f32[128,16]{1,0:T(8,128)S(1)} %copy.89, f32[129]{0:T(256)S(1)} %fusion.95, f32[128,16]{1,0:T(8,128)S(1)} %copy.91, f32[128,16]{1,0:T(8,128)S(1)} %copy.88), kind=kLoop, calls=%fused_computation.66 | loop fusion | flops 1849344 | bytes 3204104 | tf_op jit(solution)/shard_map/mul | solution.py:75
  158.9 54.5 %gather_fusion.1 = f32[16384,128]{1,0:T(8,128)} fusion(f32[128,128]{1,0:T(8,128)S(1)} %copy.92, s32[16384]{0:T(1024)S(1)} %fusion.89), kind=kCustom, calls=%fused_computation.1 | custom fusion | bytes 16842752 | tf_op jit(solution)/shard_map/jit(_take)/gather | solution.py:83
  213.4 9.3 %copy.93 = f32[128,128,128]{1,0,2:T(8,128)} copy(f32[128,128,128]{2,1,0:T(8,128)} %bitcast.211) | data formatting | bytes 16777216 | tf_op jit(solution)/shard_map/jit(_take)/gather | solution.py:83
  227.9 7.5 %select_bitcast_fusion = bf16[128,128,256]{2,1,0:T(8,128)(2,1)} fusion(bf16[128,256,128]{1,0,2:T(8,128)(2,1)} %copy.87, pred[128,256]{1,0:T(8,128)(4,1)S(1)} %get-tuple-element.472, pred[128,256]{1,0:T(8,128)(4,1)S(1)} %get-tuple-element.471), kind=kLoop, calls=%fused_computation.56 | loop fusion | flops 8388608 | bytes 16842752 | tf_op jit(solution)/shard_map/jit(_where)/select_n | solution.py:63
  235.4 6.8 %fusion.42 = bf16[128,128,128]{2,1,0:T(8,128)(2,1)} fusion(f32[128,128,128]{1,0,2:T(8,128)} %copy.93, pred[128,128]{1,0:T(8,128)(4,1)S(1)} %get-tuple-element.476, pred[128,128]{1,0:T(8,128)(4,1)S(1)} %get-tuple-element.475), kind=kLoop, calls=%fused_computation.54 | loop fusion | flops 12582912 | bytes 12615680 | tf_op jit(solution)/shard_map/convert_element_type | solution.py:97
  269.7 7.3 %collective-permute-done.1 = bf16[128,2048]{1,0:T(8,128)(2,1)S(1)} collective-permute-done((bf16[128,2048]{1,0:T(8,128)(2,1)S(1)}, bf16[128,2048]{1,0:T(8,128)(2,1)S(1)}, u32[]{:S(2)}, u32[]{:S(2)}) %collective-permute-start.1) | collective-permute-done | bytes 524320 | tf_op jit(solution)/shard_map/ppermute | solution.py:16
  280.9 15.2 %while.64 = (s32[]{:T(128)}, bf16[2,128,16,128]{3,2,1,0:T(8,128)(2,1)S(1)}, s32[2]{0:T(128)S(1)}, bf16[128,16,384]{2,1,0:T(8,128)(2,1)}, s32[256]{0:T(256)S(1)},...) while((s32[]{:T(128)}, bf16[2,128,16,128]{3,2,1,0:T(8,128)(2,1)S(1)}, ...), condition=%wide.region_5.6_spmd.clone, body=%wide.region_4.5_spmd.sunk.clone | while | flops 138706944 | bytes 10032308 | solution.py:184
  282.4 6.1 %fusion.126 = bf16[2,128,16,128]{3,2,1,0:T(8,128)(2,1)S(1)} fusion(bf16[2,128,16,128]{3,2,1,0:T(8,128)(2,1)S(1)} %get-tuple-element.826, s32[]{:T(128)} %get-tuple-element.825, bf16[128,128,256]{2,1,0:T(8,128)(2,1)} %get-tuple-element.839, pred[128,256]{1,0:T(8,128)(4,1)S(1)} %broadcast_compare_fusion.7, ...), kind=kOutput, calls=%fused_computation.8.clone.1.clone | convolution fusion | flops 138674176 | bytes 9994756 | tf_op jit(solution)/shard_map/while/body/eval_jaxpr/gts,gis->git/dot_general | solution.py:180
  290.0 6.1 %fusion.126 = bf16[2,128,16,128]{3,2,1,0:T(8,128)(2,1)S(1)} fusion(bf16[2,128,16,128]{3,2,1,0:T(8,128)(2,1)S(1)} %get-tuple-element.826, s32[]{:T(128)} %get-tuple-element.825, bf16[128,128,256]{2,1,0:T(8,128)(2,1)} %get-tuple-element.839, pred[128,256]{1,0:T(8,128)(4,1)S(1)} %broadcast_compare_fusion.7, ...), kind=kOutput, calls=%fused_computation.8.clone.1.clone | convolution fusion | flops 138674176 | bytes 9994756 | tf_op jit(solution)/shard_map/while/body/eval_jaxpr/gts,gis->git/dot_general | solution.py:180
  304.0 7.3 %while.67 = (s32[]{:T(128)}, f32[128,16]{0,1:T(8,128)S(1)}, f32[128,16]{0,1:T(8,128)S(1)}, f32[128,16,16]{0,2,1:T(8,128)S(1)}, f32[128,16,16]{0,2,1:T(8,128)S(1)...) while((s32[]{:T(128)}, f32[128,16]{0,1:T(8,128)S(1)}, ...), condition=%wide.region_11.12_spmd.clone.clone, body=%wide.region_10.11_spmd.clone.sunk.clone | while | flops 421891 | bytes 2000031 | solution.py:229
  311.3 17.7 %all-gather.2 = f32[512,16,16]{0,2,1:T(8,128)} all-gather(f32[128,16,16]{0,2,1:T(8,128)S(1)} %get-tuple-element.221), channel_id=4, replica_groups=mesh['groups'=2,'seq'=4,'chan'=2,'rep'=2] {'seq'}, dimensions={0}, use_global_device_ids=true | all-gather | bytes 655360 | tf_op jit(solution)/shard_map/all_gather | solution.py:21
  331.1 15.5 %all-gather.3 = f32[512,16,16]{0,2,1:T(8,128)} all-gather(f32[128,16,16]{0,2,1:T(8,128)S(1)} %get-tuple-element.222), channel_id=5, replica_groups=mesh['groups'=2,'seq'=4,'chan'=2,'rep'=2] {'seq'}, dimensions={0}, use_global_device_ids=true | all-gather | bytes 655360 | tf_op jit(solution)/shard_map/all_gather | solution.py:21
  348.6 13.1 %all-gather = f32[512,16]{0,1:T(8,128)S(1)} all-gather(f32[128,16]{0,1:T(8,128)S(1)} %get-tuple-element.219), channel_id=2, replica_groups=mesh['groups'=2,'seq'=4,'chan'=2,'rep'=2] {'seq'}, dimensions={0}, use_global_device_ids=true | all-gather | bytes 40960 | tf_op jit(solution)/shard_map/all_gather | solution.py:21
  361.7 13.1 %all-gather.1 = f32[512,16]{0,1:T(8,128)S(1)} all-gather(f32[128,16]{0,1:T(8,128)S(1)} %get-tuple-element.220), channel_id=3, replica_groups=mesh['groups'=2,'seq'=4,'chan'=2,'rep'=2] {'seq'}, dimensions={0}, use_global_device_ids=true | all-gather | bytes 40960 | tf_op jit(solution)/shard_map/all_gather | solution.py:21
  381.0 16.2 %while.65 = (s32[]{:T(128)}, f32[2,128,16,128]{3,2,0,1:T(8,128)}, bf16[2,128,16,128]{3,2,1,0:T(8,128)(2,1)S(1)}, s32[2,128]{1,0:T(2,128)S(1)}, bf16[128,128,128]{2,1,0:T(8,128)(2,1)}, /*index=5*/bf16[128,128,128]{2,1,0:T(8,128)(2,1)}) while((s32[]{:T(128)}, f32[2,128,16,128]{3,2,0,1:T(8,128)}, ...), condition=%wide.region_8.9_spmd.clone, body=%wide.region_7.8_spmd.sunk.clone | while | flops 138690560 | bytes 29411944 | solution.py:202
  389.3 4.6 fusion.132
  397.3 5.3 %fusion.66 = f32[128,16,2,128]{3,1,2,0:T(8,128)S(1)} fusion(f32[2,128,16,128]{3,2,0,1:T(8,128)} %get-tuple-element.216, f32[2,128,16,32]{3,2,0,1:T(8,128)} %copy.103, f32[128,128,16]{0,2,1:T(8,128)} %get-tuple-element.440, f32[128,128,16]{0,2,1:T(8,128)} %get-tuple-element.438, bf16[2,128,16,128]{3,2,1,0:T(8,128)(2,1)S(1)} %get-tuple-element.924, ...), kind=kOutput, calls=%fused_computation.96 | convolution fusion | flops 204472320 | bytes 7873536 | tf_op jit(solution)/shard_map/gtm,jgim->jgit/dot_general | solution.py:244
  405.4 5.7 %psum.28 = f32[256]{0:T(256)S(1)} all-reduce(f32[256]{0:T(256)S(1)} %fusion.43), channel_id=1, replica_groups=mesh['groups'=2,'seq'=4,'chan'=2,'rep'=2] {'chan','rep'}, use_global_device_ids=true, to_apply=%region_15.16 | all-reduce | flops 256 | bytes 2048 | tf_op jit(solution)/shard_map/psum | solution.py:260
  415.0 24.1 %all-reduce.3.cloned.1.call-done = f32[256,512]{1,0:T(8,128)} async-done(((f32[256,512]{1,0:T(8,128)}), f32[256,512]{1,0:T(8,128)}) %all-reduce.3.cloned.1.call-update) | async-done | bytes 524304 | tf_op jit(solution)/shard_map/psum | solution.py:265
  439.1 32.2 %all-reduce.5.cloned.1.call-done = f32[256,512]{1,0:T(8,128)} async-done(((f32[256,512]{1,0:T(8,128)}), f32[256,512]{1,0:T(8,128)}) %all-reduce.5.cloned.1.call-update) | async-done | bytes 524304 | tf_op jit(solution)/shard_map/psum | solution.py:266
  472.7 11.7 %psum.31 = f32[8]{0:T(128)S(1)} all-reduce(f32[8]{0:T(128)S(1)} %select_reduce_fusion.1), channel_id=1, replica_groups=mesh['groups'=2,'seq'=4,'chan'=2,'rep'=2] {'seq'}, use_global_device_ids=true, to_apply=%region_21.22 | all-reduce | flops 8 | bytes 64 | tf_op jit(solution)/shard_map/psum | solution.py:277
  (195 shorter events, 93.2 us)
Async XLA Ops:
  7.2 403.9 %copy-start = (bf16[2048,512]{1,0:T(8,128)(2,1)S(1)}, bf16[2048,512]{1,0:T(8,128)(2,1)}, u32[]{:S(2)}) copy-start(bf16[2048,512]{1,0:T(8,128)(2,1)} %param.27) | copy-start | bytes 6291460
  7.2 13.0 %copy-start.1 = (bf16[128,128]{1,0:T(8,128)(2,1)S(1)}, bf16[128,128]{1,0:T(8,128)(2,1)}, u32[]{:S(2)}) copy-start(bf16[128,128]{1,0:T(8,128)(2,1)} %param.23) | copy-start | bytes 98308
  7.2 431.9 %all-reduce.3.cloned.1.call-start = ((), (), s32[]{:S(2)}) async-start(), calls=%async_computation | async-start | bytes 1048576 | tf_op jit(solution)/shard_map/psum | solution.py:265
  8.8 248.4 %collective-permute-start = (bf16[2,8,2048]{2,1,0:T(8,128)(2,1)}, bf16[2,8,2048]{2,1,0:T(8,128)(2,1)}, u32[]{:S(2)}, u32[]{:S(2)}) collective-permute-start(bf16[2,8,2048]{2,1,0:T(8,128)(2,1)} %pad_maximum_fusion.1), channel_id=1, source_target_pairs={{0,4},{4,8},{8,12},{1,5},{5,9},{9,13},{2,6},{6,10},{10,14},{3,7},{... | collective-permute-start | bytes 196616 | tf_op jit(solution)/shard_map/ppermute | solution.py:16
  19.4 128.2 %copy-start.28 = (s32[2,128]{1,0:T(2,128)}, s32[2,128]{1,0:T(2,128)S(1)}, u32[]{:S(2)}) copy-start(s32[2,128]{1,0:T(2,128)S(1)} %get-tuple-element.844) | copy-start | bytes 3076
  134.3 12.9 %copy-start.13 = (f32[4,128,16]{1,2,0:T(8,128)S(1)}, f32[4,128,16]{1,2,0:T(8,128)}, u32[]{:S(2)}) copy-start(f32[4,128,16]{1,2,0:T(8,128)} %param.24) | copy-start | bytes 98308
  260.0 6.3 %slice-start = ((s8[8388608]{0:T(1024)(128)(4,1)}), s8[4194304]{0:T(1024)(128)(4,1)S(1)}, s32[]{:S(2)}) async-start(s8[8388608]{0:T(1024)(128)(4,1)} %bitcast.208), calls=%async_computation.2 | async-start | bytes 8388608
  260.1 6.2 %slice-start.1 = ((s8[8388608]{0:T(1024)(128)(4,1)}), s8[4194304]{0:T(1024)(128)(4,1)S(1)}, s32[]{:S(2)}) async-start(s8[8388608]{0:T(1024)(128)(4,1)} %bitcast.208), calls=%async_computation.3 | async-start | bytes 8388608
  263.2 13.8 %collective-permute-start.1 = (bf16[128,2048]{1,0:T(8,128)(2,1)S(1)}, bf16[128,2048]{1,0:T(8,128)(2,1)S(1)}, u32[]{:S(2)}, u32[]{:S(2)}) collective-permute-start(bf16[128,2048]{1,0:T(8,128)(2,1)S(1)} %slice.177), channel_id=1, source_target_pairs={{0,4},{4,8},{8,12},{1,5},{5,9},{9,13},{2,6},{6,10},{10,14},{3,7},{... | collective-permute-start | bytes 1572872 | tf_op jit(solution)/shard_map/ppermute | solution.py:16
  278.2 2.6 copy-start.14
  278.2 2.6 copy-start.24
  280.9 15.2 %copy-start.16 = (pred[2,128]{1,0:T(4,128)(4,1)S(1)}, pred[2,128]{1,0:T(4,128)(4,1)}, u32[]{:S(2)}) copy-start(pred[2,128]{1,0:T(4,128)(4,1)} %get-tuple-element.468) | copy-start | bytes 772
  300.5 3.5 copy-start.15
  300.5 3.5 copy-start.32
  376.2 4.8 copy-start.29
  381.0 16.2 %copy-start.17 = (f32[2,128]{1,0:T(2,128)S(1)}, f32[2,128]{1,0:T(2,128)}, u32[]{:S(2)}) copy-start(f32[2,128]{1,0:T(2,128)} %get-tuple-element.467) | copy-start | bytes 3076
  381.1 4.6 copy-start.6
  389.3 4.6 copy-start.6
  403.7 7.3 %copy-start.30 = (f32[2048]{0:T(1024)S(1)}, f32[2048]{0:T(1024)}, u32[]{:S(2)}) copy-start(f32[2048]{0:T(1024)} %param.26) | copy-start | bytes 24580
  411.1 60.2 %copy-start.27 = (s32[256]{0:T(256)S(1)}, s32[256]{0:T(256)}, u32[]{:S(2)}) copy-start(s32[256]{0:T(256)} %param.28) | copy-start | bytes 3076
  411.1 61.5 %copy-start.25 = (s32[256]{0:T(256)S(1)}, s32[256]{0:T(256)}, u32[]{:S(2)}) copy-start(s32[256]{0:T(256)} %get-tuple-element.821) | copy-start | bytes 3076
  411.1 73.3 %copy-start.31 = (s32[8]{0:T(128)S(1)}, s32[8]{0:T(128)}, u32[]{:S(2)}) copy-start(s32[8]{0:T(128)} %param.29) | copy-start | bytes 100
  414.9 56.3 %all-reduce.5.cloned.1.call-start = ((), (), s32[]{:S(2)}) async-start(), calls=%async_computation.1 | async-start | bytes 1048576 | tf_op jit(solution)/shard_map/psum | solution.py:266
  472.6 12.3 %copy-start.26 = (f32[256]{0:T(256)}, f32[256]{0:T(256)S(1)}, u32[]{:S(2)}) copy-start(f32[256]{0:T(256)S(1)} %log_subtract_fusion) | copy-start | bytes 3076
  (16 other events, 33.6 us)
Sparse Core Ops, SparseCore 0:
  415.1 23.9 all-reduce.2
  441.5 29.7 all-reduce.4
